TPU v7x, 32 devices: a whole 2x2x4 slice. The times are simulated.
32 devices in a mesh: gx: 4 (over x, core), gy: 8 (over z, y).
Axes of the slice: x: 2, y: 2, z: 4, core: 2. Of those that a mesh axis runs over, the one named last changes fastest.
Arguments:
- right_side: float32 [4, 1024, 2048], P(None, 'gx', 'gy')
- prior_weight: float32 [4, 1024, 2048], P(None, 'gx', 'gy'), may hold values from 0.5 to 4
- jacobi_inverse: float32 [4, 1024, 2048], P(None, 'gx', 'gy'), may hold values from 0.1 to 0.5
- interaction: float32 [2, 4, 128, 128], replicated, may hold values from -0.5 to 0.5
- footprint: int32 [2, 16, 16, 4], P(None, 'gx', 'gy'), may hold values from 0 to 255, as said below
Outputs:
- solution: float32 [4, 1024, 2048], P(None, 'gx', 'gy')
- residual: float32 [4, 1024, 2048], P(None, 'gx', 'gy')
Inputs may be any that keep to these rules, and one draw needn't show every extreme that they name: `footprint`: each entry is bx * 16 + by of a block of the same 4 block rows along the first dimension as its ray block's tile. Of the 64 entries of one tile's ray blocks, between 7 and 9 fall in each tile of the same strip along the second dimension, exactly 9 in some; one tile of the second dimension receives exactly 9 entries from every tile of the strip.
All inputs are finite; a program needn't handle non-finite values.
Results may differ from a plain program's by a relative error of at most 0.0003.
Values sent between devices are 32-bit elements; how exact they have to be, the bound alone decides.
No kernel may reach another device: no remote copies, remote signals or barrier semaphores. Data moves between devices by JAX's collectives and lax.ppermute only.
A program may use at most 128 MiB of HBM per device.

v0:
```python
import jax
import jax.numpy as jnp
from jax import lax
from jax.sharding import PartitionSpec as P

ITERS = 4
DAUB_LOW = (
    0.3326705529509569,
    0.8068915093133388,
    0.4598775021193313,
    -0.13501102001039084,
    -0.08544127388224149,
    0.035226291882100656,
)
DAUB_HIGH = tuple(((-1.0) ** tap_index * DAUB_LOW[5 - tap_index] for tap_index in range(6)))


def extended(block, sides, width):
    for axis, dim in sides:
        count = lax.axis_size(axis)
        forward = [(i, i + 1) for i in range(count - 1)]
        backward = [(target, source) for source, target in forward]
        low = lax.ppermute(
            lax.slice_in_dim(block, block.shape[dim] - width, None, axis=dim), axis, forward
        )
        high = lax.ppermute(lax.slice_in_dim(block, 0, width, axis=dim), axis, backward)
        block = jnp.concatenate([low, block, high], axis=dim)
    return block


def synth_table(length):
    inputs = jnp.arange(length + 8, dtype=jnp.int32)[:, None]
    outputs = jnp.arange(length, dtype=jnp.int32)[None, :]
    half = outputs // 2
    phase = outputs % 2
    table = jnp.zeros((length + 8, length), jnp.float32)
    for tap_num in range(3):
        low_coef = jnp.where(phase == 0, DAUB_LOW[2 * tap_num], DAUB_LOW[2 * tap_num + 1])
        high_coef = jnp.where(phase == 0, DAUB_HIGH[2 * tap_num], DAUB_HIGH[2 * tap_num + 1])
        table = table + jnp.where(inputs == 2 * (half - tap_num) + 4, low_coef, 0.0)
        table = table + jnp.where(inputs == 2 * (half - tap_num) + 5, high_coef, 0.0)
    return table


def analysis_table(length):
    inputs = jnp.arange(length + 8, dtype=jnp.int32)[:, None]
    outputs = jnp.arange(length, dtype=jnp.int32)[None, :]
    half = outputs // 2
    phase = outputs % 2
    table = jnp.zeros((length + 8, length), jnp.float32)
    for tap_num in range(3):
        for offset in (0, 1):
            coef = jnp.where(
                phase == 0, DAUB_LOW[2 * tap_num + offset], DAUB_HIGH[2 * tap_num + offset]
            )
            table = table + jnp.where(inputs == 2 * (half + tap_num) + offset + 4, coef, 0.0)
    return table


def butterfly_sum(value, axis):
    count = lax.axis_size(axis)
    if count & count - 1:
        return lax.psum(value, axis)
    stride = 1
    while stride < count:
        value = value + lax.ppermute(value, axis, [(i, i ^ stride) for i in range(count)])
        stride *= 2
    return value


def global_sum(local_value):
    return butterfly_sum(butterfly_sum(local_value, "gx"), "gy")


def with_rim(field):
    return extended(field, (("gx", 1), ("gy", 2)), 4)


def shards(right_side, prior_weight, jacobi_inverse, interaction, footprint):
    highest = lax.Precision.HIGHEST
    layers, tile_rows, tile_cols = right_side.shape
    sensors, rows_blocks, cols_blocks = (footprint.shape[0], footprint.shape[1], footprint.shape[2])
    block_rows = tile_rows // rows_blocks
    block_cols = tile_cols // cols_blocks
    owners = lax.axis_size("gy")
    layer_blocks_cols = cols_blocks * owners
    requests = sensors * rows_blocks * cols_blocks * layers
    capacity = requests // owners + 1
    own_blocks = layers * rows_blocks * cols_blocks
    synth_rows = synth_table(tile_rows)
    synth_cols = synth_table(tile_cols)
    analysis_rows = analysis_table(tile_rows)
    analysis_cols = analysis_table(tile_cols)
    flat_ids = footprint.reshape(requests)
    request_num = jnp.arange(requests, dtype=jnp.int32)
    layer_of = request_num % layers
    sensor_of = request_num // (requests // sensors)
    target = flat_ids % layer_blocks_cols // cols_blocks
    owned_index = (
        layer_of * (rows_blocks * cols_blocks)
        + flat_ids // layer_blocks_cols % rows_blocks * cols_blocks
        + flat_ids % layer_blocks_cols % cols_blocks
    )
    picks = (target[:, None] == jnp.arange(owners, dtype=jnp.int32)[None, :]).astype(jnp.int32)
    slot = jnp.sum(picks * (jnp.cumsum(picks, axis=0) - 1), axis=1)
    send_ids = jnp.full((owners, capacity), own_blocks, jnp.int32).at[target, slot].set(owned_index)
    send_pairs = (
        jnp.zeros((owners, capacity), jnp.int32).at[target, slot].set(sensor_of * layers + layer_of)
    )
    wanted_ids, wanted_pairs = (
        lax.all_to_all(send_ids, "gy", split_axis=0, concat_axis=0, tiled=True),
        lax.all_to_all(send_pairs, "gy", split_axis=0, concat_axis=0, tiled=True),
    )
    slot_source = (
        jnp.full((owners, capacity), requests, jnp.int32).at[target, slot].set(request_num)
    )
    landing = (
        wanted_ids.reshape(-1)[None, :] == jnp.arange(own_blocks, dtype=jnp.int32)[:, None]
    ).astype(jnp.float32)

    def apply_op(direction):
        synthesize_padded = with_rim(direction)
        along_rows = jnp.einsum("lab,ac->lcb", synthesize_padded, synth_rows, precision=highest)
        blocks = (
            jnp.einsum("lab,bc->lac", along_rows, synth_cols, precision=highest)
            .reshape(layers, rows_blocks, block_rows, cols_blocks, block_cols)
            .transpose(0, 1, 3, 2, 4)
            .reshape(own_blocks, block_rows, block_cols)
        )
        outgoing = jnp.take(blocks, wanted_ids, axis=0, mode="fill", fill_value=0.0)
        arrived = lax.all_to_all(outgoing, "gy", split_axis=0, concat_axis=0, tiled=True)
        seen = arrived[target, slot].reshape(
            sensors, rows_blocks * cols_blocks, layers, block_rows, block_cols
        )
        slopes = jnp.einsum("sklxy,slyz->skxz", seen, interaction, precision=highest)
        back = jnp.einsum("skxz,slyz->sklxy", slopes, interaction, precision=highest).reshape(
            requests, block_rows, block_cols
        )
        returning = jnp.take(back, slot_source, axis=0, mode="fill", fill_value=0.0)
        landed = lax.all_to_all(returning, "gy", split_axis=0, concat_axis=0, tiled=True)
        summed = jnp.dot(
            landing, landed.reshape(owners * capacity, block_rows * block_cols), precision=highest
        )
        padded = with_rim(
            summed.reshape(layers, rows_blocks, cols_blocks, block_rows, block_cols)
            .transpose(0, 1, 3, 2, 4)
            .reshape(layers, tile_rows, tile_cols)
        )
        along_cols = jnp.einsum("lab,bc->lac", padded, analysis_cols, precision=highest)
        return (
            jnp.einsum("lab,ac->lcb", along_cols, analysis_rows, precision=highest)
            + prior_weight * direction
        )

    solution = jnp.zeros_like(right_side)
    residual = right_side
    precond_res = jacobi_inverse * residual
    direction = precond_res
    rho_now = global_sum(jnp.sum(residual * precond_res))
    image = apply_op(direction)
    for step in range(ITERS):
        step_size = rho_now / global_sum(jnp.sum(direction * image))
        solution = solution + step_size * direction
        residual = residual - step_size * image
        if step + 1 < ITERS:
            precond_res = jacobi_inverse * residual
            rho_next = global_sum(jnp.sum(residual * precond_res))
            applied = apply_op(precond_res)
            ratio = rho_next / rho_now
            direction = precond_res + ratio * direction
            image = applied + ratio * image
            rho_now = rho_next
    return (solution, residual)


def solution(mesh):
    return jax.shard_map(
        shards,
        mesh=mesh,
        in_specs=(
            P(None, "gx", "gy"),
            P(None, "gx", "gy"),
            P(None, "gx", "gy"),
            P(),
            P(None, "gx", "gy", None),
        ),
        out_specs=(P(None, "gx", "gy"), P(None, "gx", "gy")),
        check_vma=False,
    )
```

profile of v0, /device:TPU:0, one launch (start us, length us, event | category | flops | bytes accessed | tf_op | source)
XLA Modules:
  0.0 1004.9 jit_solution(15432480952967989075)
XLA Ops:
  3.4 10.1 %scatter_fusion = s32[8,9]{1,0:T(8,128)} fusion(s32[8,9]{1,0:T(8,128)} %broadcast_in_dim.425, s32[64]{0:T(128)S(1)} %fusion.183, s32[64]{0:T(128)S(1)} %get-tuple-element.21), kind=kCustom, calls=%fused_computation.12 | custom fusion | bytes 1280 | tf_op jit(solution)/shard_map/scatter | solution.py:106
  13.5 7.3 all-to-all-start
  33.4 3.9 collective-permute-start.7
  38.9 4.2 collective-permute-done.8
  56.5 6.0 all-to-all-start.1
  66.1 48.2 %all-to-all-done.1 = f32[8,9,64,128]{3,2,1,0:T(8,128)} async-done(((f32[8,9,64,128]{3,2,1,0:T(8,128)}), f32[8,9,64,128]{3,2,1,0:T(8,128)}, u32[]{:S(2)}, u32[]{:S(2)}) %all-to-all-start.1) | async-done | bytes 2359328 | tf_op jit(solution)/shard_map/all_to_all | solution.py:131
  131.6 7.1 all-to-all-start.2
  139.9 54.4 %all-to-all-done.2 = f32[8,9,64,128]{3,2,1,0:T(8,128)} async-done(((f32[8,9,64,128]{3,2,1,0:T(8,128)}), f32[8,9,64,128]{3,2,1,0:T(8,128)}, u32[]{:S(2)}, u32[]{:S(2)}) %all-to-all-start.2) | async-done | bytes 2359328 | tf_op jit(solution)/shard_map/all_to_all | solution.py:140
  213.5 4.5 collective-permute-start.11
  221.0 3.8 fusion.18
  224.8 4.5 multiply_reduce_fusion.6
  245.7 4.1 collective-permute-start.16
  254.6 4.0 collective-permute-start.4
  266.6 4.1 collective-permute-done.24
  275.0 4.9 collective-permute-done.26
  282.3 3.8 fusion.199
  296.3 59.0 %all_to_all.52 = f32[8,9,64,128]{3,2,1,0:T(8,128)} all-to-all(f32[8,9,64,128]{3,2,1,0:T(8,128)S(1)} %broadcast_select_fusion.5), channel_id=1, replica_groups=mesh['gx'=4,'gy'=8] {'gy'}, dimensions={0} | all-to-all | bytes 4718592 | tf_op jit(solution)/shard_map/all_to_all | solution.py:131
  371.3 59.9 %all_to_all.53 = f32[8,9,64,128]{3,2,1,0:T(8,128)S(1)} all-to-all(f32[8,9,64,128]{3,2,1,0:T(8,128)S(1)} %broadcast_select_fusion.4), channel_id=1, replica_groups=mesh['gx'=4,'gy'=8] {'gy'}, dimensions={0} | all-to-all | bytes 4718592 | tf_op jit(solution)/shard_map/all_to_all | solution.py:140
  479.4 3.8 fusion.38
  483.2 4.6 multiply_reduce_fusion.4
  523.4 4.2 collective-permute-done.44
  530.0 3.8 fusion.196
  544.0 56.9 %all_to_all.54 = f32[8,9,64,128]{3,2,1,0:T(8,128)} all-to-all(f32[8,9,64,128]{3,2,1,0:T(8,128)S(1)} %broadcast_select_fusion.3), channel_id=1, replica_groups=mesh['gx'=4,'gy'=8] {'gy'}, dimensions={0} | all-to-all | bytes 4718592 | tf_op jit(solution)/shard_map/all_to_all | solution.py:131
  616.8 59.8 %all_to_all.55 = f32[8,9,64,128]{3,2,1,0:T(8,128)S(1)} all-to-all(f32[8,9,64,128]{3,2,1,0:T(8,128)S(1)} %broadcast_select_fusion.2), channel_id=1, replica_groups=mesh['gx'=4,'gy'=8] {'gy'}, dimensions={0} | all-to-all | bytes 4718592 | tf_op jit(solution)/shard_map/all_to_all | solution.py:140
  724.5 3.9 fusion.58
  728.4 5.2 multiply_reduce_fusion.2
  769.4 3.9 collective-permute-done.62
  775.7 3.8 fusion.193
  789.7 56.9 %all_to_all.56 = f32[8,9,64,128]{3,2,1,0:T(8,128)} all-to-all(f32[8,9,64,128]{3,2,1,0:T(8,128)S(1)} %broadcast_select_fusion.1), channel_id=1, replica_groups=mesh['gx'=4,'gy'=8] {'gy'}, dimensions={0} | all-to-all | bytes 4718592 | tf_op jit(solution)/shard_map/all_to_all | solution.py:131
  862.6 59.7 %all_to_all.57 = f32[8,9,64,128]{3,2,1,0:T(8,128)S(1)} all-to-all(f32[8,9,64,128]{3,2,1,0:T(8,128)S(1)} %broadcast_select_fusion), channel_id=1, replica_groups=mesh['gx'=4,'gy'=8] {'gy'}, dimensions={0} | all-to-all | bytes 4718592 | tf_op jit(solution)/shard_map/all_to_all | solution.py:140
  970.1 3.9 fusion.78
  974.0 4.6 multiply_reduce_fusion
  (319 shorter events, 404.5 us)
Async XLA Ops:
  13.5 15.8 %all-to-all-start = ((s32[8,1,9]{2,1,0:T(1,128)}), s32[8,1,9]{2,1,0:T(1,128)S(1)}, u32[]{:S(2)}, u32[]{:S(2)}) async-start(s32[8,1,9]{2,1,0:T(1,128)} %bitcast.4), calls=%async_computation | async-start | bytes 8192 | tf_op jit(solution)/shard_map/all_to_all | solution.py:111
  28.0 5.3 collective-permute-start.6
  33.4 5.4 collective-permute-start.7
  37.4 5.7 collective-permute-start.8
  56.5 57.7 %all-to-all-start.1 = ((f32[8,9,64,128]{3,2,1,0:T(8,128)}), f32[8,9,64,128]{3,2,1,0:T(8,128)}, u32[]{:S(2)}, u32[]{:S(2)}) async-start(f32[8,9,64,128]{3,2,1,0:T(8,128)} %broadcast_select_fusion.7), calls=%async_computation.1 | async-start | bytes 4718592 | tf_op jit(solution)/shard_map/all_to_all | solution.py:131
  131.6 62.8 %all-to-all-start.2 = ((f32[8,9,64,128]{3,2,1,0:T(8,128)}), f32[8,9,64,128]{3,2,1,0:T(8,128)}, u32[]{:S(2)}, u32[]{:S(2)}) async-start(f32[8,9,64,128]{3,2,1,0:T(8,128)} %broadcast_select_fusion.6), calls=%async_computation.2 | async-start | bytes 4718592 | tf_op jit(solution)/shard_map/all_to_all | solution.py:140
  212.2 7.7 collective-permute-start.12
  213.5 6.1 collective-permute-start.11
  233.1 5.9 collective-permute-start.14
  236.4 6.6 collective-permute-start.1
  239.8 5.4 collective-permute-start.15
  243.7 6.1 collective-permute-start.2
  245.7 6.1 collective-permute-start.16
  252.3 6.3 collective-permute-start.17
  254.6 4.6 collective-permute-start.4
  265.1 5.6 collective-permute-start.24
  273.5 6.5 collective-permute-start.26
  450.0 28.0 %collective-permute-start.29 = (f32[4,264,4]{1,2,0:T(4,128)S(1)}, f32[4,264,4]{1,2,0:T(4,128)S(1)}, u32[]{:S(2)}, u32[]{:S(2)}) collective-permute-start(f32[4,264,4]{1,2,0:T(4,128)S(1)} %copy.37), channel_id=1, source_target_pairs={{0,1},{1,2},{2,3},{3,4},{4,5},{5,6},{6,7},{8,9},{9,10},{10,11},{11... | collective-permute-start | bytes 50696 | tf_op jit(solution)/shard_map/ppermute | solution.py:23
  453.6 24.7 %collective-permute-start.30 = (f32[4,264,4]{1,2,0:T(4,128)S(1)}, f32[4,264,4]{1,2,0:T(4,128)S(1)}, u32[]{:S(2)}, u32[]{:S(2)}) collective-permute-start(f32[4,264,4]{1,2,0:T(4,128)S(1)} %copy.38), channel_id=1, source_target_pairs={{1,0},{2,1},{3,2},{4,3},{5,4},{6,5},{7,6},{9,8},{10,9},{11,10},{12... | collective-permute-start | bytes 50696 | tf_op jit(solution)/shard_map/ppermute | solution.py:26
  472.8 4.6 collective-permute-start.22
  513.2 4.8 collective-permute-start.42
  518.1 5.2 collective-permute-start.43
  521.9 5.7 collective-permute-start.44
  695.4 27.7 %collective-permute-start.47 = (f32[4,264,4]{1,2,0:T(4,128)S(1)}, f32[4,264,4]{1,2,0:T(4,128)S(1)}, u32[]{:S(2)}, u32[]{:S(2)}) collective-permute-start(f32[4,264,4]{1,2,0:T(4,128)S(1)} %copy.47), channel_id=1, source_target_pairs={{0,1},{1,2},{2,3},{3,4},{4,5},{5,6},{6,7},{8,9},{9,10},{10,11},{11... | collective-permute-start | bytes 50696 | tf_op jit(solution)/shard_map/ppermute | solution.py:23
  699.0 24.4 %collective-permute-start.48 = (f32[4,264,4]{1,2,0:T(4,128)S(1)}, f32[4,264,4]{1,2,0:T(4,128)S(1)}, u32[]{:S(2)}, u32[]{:S(2)}) collective-permute-start(f32[4,264,4]{1,2,0:T(4,128)S(1)} %copy.48), channel_id=1, source_target_pairs={{1,0},{2,1},{3,2},{4,3},{5,4},{6,5},{7,6},{9,8},{10,9},{11,10},{12... | collective-permute-start | bytes 50696 | tf_op jit(solution)/shard_map/ppermute | solution.py:26
  717.9 4.6 collective-permute-start.40
  759.0 4.8 collective-permute-start.60
  763.9 5.5 collective-permute-start.61
  767.6 5.7 collective-permute-start.62
  941.1 27.7 %collective-permute-start.65 = (f32[4,264,4]{1,2,0:T(4,128)S(1)}, f32[4,264,4]{1,2,0:T(4,128)S(1)}, u32[]{:S(2)}, u32[]{:S(2)}) collective-permute-start(f32[4,264,4]{1,2,0:T(4,128)S(1)} %copy.57), channel_id=1, source_target_pairs={{0,1},{1,2},{2,3},{3,4},{4,5},{5,6},{6,7},{8,9},{9,10},{10,11},{11... | collective-permute-start | bytes 50696 | tf_op jit(solution)/shard_map/ppermute | solution.py:23
  944.7 24.3 %collective-permute-start.66 = (f32[4,264,4]{1,2,0:T(4,128)S(1)}, f32[4,264,4]{1,2,0:T(4,128)S(1)}, u32[]{:S(2)}, u32[]{:S(2)}) collective-permute-start(f32[4,264,4]{1,2,0:T(4,128)S(1)} %copy.58), channel_id=1, source_target_pairs={{1,0},{2,1},{3,2},{4,3},{5,4},{6,5},{7,6},{9,8},{10,9},{11,10},{12... | collective-permute-start | bytes 50696 | tf_op jit(solution)/shard_map/ppermute | solution.py:26
  963.6 4.6 collective-permute-start.58
  (63 other events, 375.8 us)
where the time goes:
time: 1020 us; the launch traced here: 1000 us
  blocking collectives  352 us (35%)
  starting transfers between devices  187 us (18%)
  waiting for transfers between devices  169 us (17%)
  local copies, waits for them, and re-layouts  130 us (13%)
  matrix products  95 us (9%)
  other arithmetic  39.3 us (4%)
  between operations  31.5 us (3%)
    all_to_all x3, blocking collectives, apply_op(): lax.all_to_all(returning, 'gy', split_axis=0, concat_axis=0, tiled=True)  179 us
    all_to_all x3, blocking collectives, apply_op(): lax.all_to_all(outgoing, 'gy', split_axis=0, concat_axis=0, tiled=True)  173 us
    ppermute x40, starting transfers between devices, butterfly_sum(): lax.ppermute(value, axis, [(i, i ^ stride) for i in range(count)])  102 us
    all_to_all x1, waiting for transfers between devices, apply_op(): lax.all_to_all(returning, 'gy', split_axis=0, concat_axis=0, tiled=True)  54.4 us
    all_to_all x1, waiting for transfers between devices, apply_op(): lax.all_to_all(outgoing, 'gy', split_axis=0, concat_axis=0, tiled=True)  48.2 us
    ppermute x16, starting transfers between devices, extended(): lax.ppermute(lax.slice_in_dim(block, block.shape[dim] - width, None, axis...  42.1 us
    ppermute x16, waiting for transfers between devices, extended(): lax.ppermute(lax.slice_in_dim(block, 0, width, axis=dim), axis, backward)  38.6 us
    ppermute x40, waiting for transfers between devices, butterfly_sum(): lax.ppermute(value, axis, [(i, i ^ stride) for i in range(count)])  26.9 us
  transfers between devices with their start and end apart: 75, of which 50 were waited for; matrix products, arithmetic and copies ran while one was open for 1% of the time, Pallas kernels for 0%

commit v1 on v0

--- a/solution.py
+++ b/solution.py
@@ -13,6 +13,17 @@
     0.035226291882100656,
 )
 DAUB_HIGH = tuple(((-1.0) ** tap_index * DAUB_LOW[5 - tap_index] for tap_index in range(6)))
+
+
+def in_blocks(array, dim, devices):
+    before, after = (array.shape[:dim], array.shape[dim + 1 :])
+    return jnp.moveaxis(array.reshape(*before, devices, -1, *after), dim, 0)
+
+
+def joined_along(tiles, dim):
+    dims = list(tiles.shape[1:])
+    dims[dim] *= tiles.shape[0]
+    return jnp.moveaxis(tiles, 0, dim).reshape(dims)
 
 
 def extended(block, sides, width):
@@ -128,7 +139,15 @@
             .reshape(own_blocks, block_rows, block_cols)
         )
         outgoing = jnp.take(blocks, wanted_ids, axis=0, mode="fill", fill_value=0.0)
-        arrived = lax.all_to_all(outgoing, "gy", split_axis=0, concat_axis=0, tiled=True)
+        size, here = (lax.axis_size("gy"), lax.axis_index("gy"))
+        tiles = in_blocks(outgoing, 0, size)
+        out = tiles
+        for k in range(1, size):
+            target_2, source_2 = ((here + k) % size, (here - k) % size)
+            sent = lax.dynamic_index_in_dim(tiles, target_2, 0)
+            other = lax.ppermute(sent, "gy", [(i_2, (i_2 + k) % size) for i_2 in range(size)])
+            out = lax.dynamic_update_slice_in_dim(out, other, source_2, axis=0)
+        arrived = joined_along(out, 0)
         seen = arrived[target, slot].reshape(
             sensors, rows_blocks * cols_blocks, layers, block_rows, block_cols
         )

time: 1020 us -> 1060 us (1.039)
  blocking collectives: 352 us -> 171 us
  waiting for transfers between devices: 169 us -> 327 us
  local copies, waits for them, and re-layouts: 130 us -> 163 us
  starting transfers between devices: 187 us -> 217 us
    ppermute x0 -> x28, waiting for transfers between devices: none -> 211 us  [apply_op(): lax.ppermute(sent, 'gy', [(i_2, (i_2 + k) % size) for i_2 in range(size)])]
    all_to_all x3 -> x0, blocking collectives: 173 us -> none  [apply_op(): lax.all_to_all(outgoing, 'gy', split_axis=0, concat_axis=0, tiled=True)]
    all_to_all x1 -> x0, waiting for transfers between devices: 48.2 us -> none  [apply_op(): lax.all_to_all(outgoing, 'gy', split_axis=0, concat_axis=0, tiled=True)]
    ppermute x0 -> x28, starting transfers between devices: none -> 39.3 us  [apply_op(): lax.ppermute(sent, 'gy', [(i_2, (i_2 + k) % size) for i_2 in range(size)])]
    dynamic_update_slice x0 -> x24, local copies, waits for them, and re-layouts: none -> 18.5 us  [apply_op(): out = lax.dynamic_update_slice_in_dim(out, other, source_2, axis=0)]
    dynamic_slice x0 -> x8, local copies, waits for them, and re-layouts: none -> 12.2 us  [apply_op(): sent = lax.dynamic_index_in_dim(tiles, target_2, 0)]
  transfers between devices with their start and end apart: 75 -> 102, of which waited for: 50 -> 66; matrix products, arithmetic and copies ran while one was open for 1% -> 3% of each run, Pallas kernels for 0% -> 0%
where the time goes in v1:
time: 1060 us; the launch traced here: 1050 us
  waiting for transfers between devices  327 us (31%)
  starting transfers between devices  217 us (20%)
  blocking collectives  171 us (16%)
  local copies, waits for them, and re-layouts  163 us (15%)
  matrix products  95.2 us (9%)
  other arithmetic  42.5 us (4%)
  between operations  32.2 us (3%)
    ppermute x28, waiting for transfers between devices, apply_op(): lax.ppermute(sent, 'gy', [(i_2, (i_2 + k) % size) for i_2 in range(size)])  211 us
    all_to_all x3, blocking collectives, apply_op(): lax.all_to_all(returning, 'gy', split_axis=0, concat_axis=0, tiled=True)  171 us
    ppermute x40, starting transfers between devices, butterfly_sum(): lax.ppermute(value, axis, [(i, i ^ stride) for i in range(count)])  105 us
    all_to_all x1, waiting for transfers between devices, apply_op(): lax.all_to_all(returning, 'gy', split_axis=0, concat_axis=0, tiled=True)  53 us
    ppermute x16, starting transfers between devices, extended(): lax.ppermute(lax.slice_in_dim(block, block.shape[dim] - width, None, axis...  39.8 us
    ppermute x28, starting transfers between devices, apply_op(): lax.ppermute(sent, 'gy', [(i_2, (i_2 + k) % size) for i_2 in range(size)])  39.3 us
    ppermute x16, waiting for transfers between devices, extended(): lax.ppermute(lax.slice_in_dim(block, 0, width, axis=dim), axis, backward)  38.5 us
    ppermute x40, waiting for transfers between devices, butterfly_sum(): lax.ppermute(value, axis, [(i, i ^ stride) for i in range(count)])  23.2 us
  transfers between devices with their start and end apart: 102, of which 66 were waited for; matrix products, arithmetic and copies ran while one was open for 3% of the time, Pallas kernels for 0%

profile of v1, /device:TPU:0, one launch (start us, length us, event | category | flops | bytes accessed | tf_op | source)
XLA Modules:
  0.0 1048.3 jit_solution(16029078282045136982)
XLA Ops:
  3.4 10.2 scatter_fusion
  13.6 7.3 all-to-all-start
  38.6 4.2 collective-permute-done.8
  78.1 13.7 %collective-permute-done.11 = f32[1,1,9,64,128]{4,3,2,1,0:T(8,128)} collective-permute-done((f32[1,1,9,64,128]{4,3,2,1,0:T(8,128)S(1)}, f32[1,1,9,64,128]{4,3,2,1,0:T(8,128)}, u32[]{:S(2)}, u32[]{:S(2)}) %collective-permute-start.11) | collective-permute-done | bytes 294944 | tf_op jit(solution)/shard_map/ppermute | solution.py:148
  93.5 30.7 %collective-permute-done.12 = f32[1,1,9,64,128]{4,3,2,1,0:T(8,128)S(1)} collective-permute-done((f32[1,1,9,64,128]{4,3,2,1,0:T(8,128)S(1)}, f32[1,1,9,64,128]{4,3,2,1,0:T(8,128)S(1)}, u32[]{:S(2)}, u32[]{:S(2)}) %collective-permute-start.12) | collective-permute-done | bytes 294944 | tf_op jit(solution)/shard_map/ppermute | solution.py:148
  144.5 4.4 all-to-all-start.1
  150.3 53.0 %all-to-all-done.1 = f32[8,9,64,128]{3,2,1,0:T(8,128)} async-done(((f32[8,9,64,128]{3,2,1,0:T(8,128)}), f32[8,9,64,128]{3,2,1,0:T(8,128)}, u32[]{:S(2)}, u32[]{:S(2)}) %all-to-all-start.1) | async-done | bytes 2359328 | tf_op jit(solution)/shard_map/all_to_all | solution.py:159
  221.7 5.0 collective-permute-start.18
  233.4 4.6 multiply_reduce_fusion.6
  284.4 4.6 collective-permute-done.33
  310.8 6.5 collective-permute-done.34
  329.0 14.5 %collective-permute-done.36 = f32[1,1,9,64,128]{4,3,2,1,0:T(8,128)S(1)} collective-permute-done((f32[1,1,9,64,128]{4,3,2,1,0:T(8,128)S(1)}, f32[1,1,9,64,128]{4,3,2,1,0:T(8,128)S(1)}, u32[]{:S(2)}, u32[]{:S(2)}) %collective-permute-start.36) | collective-permute-done | bytes 294944 | tf_op jit(solution)/shard_map/ppermute | solution.py:148
  344.2 31.3 %collective-permute-done.37 = f32[1,1,9,64,128]{4,3,2,1,0:T(8,128)S(1)} collective-permute-done((f32[1,1,9,64,128]{4,3,2,1,0:T(8,128)S(1)}, f32[1,1,9,64,128]{4,3,2,1,0:T(8,128)S(1)}, u32[]{:S(2)}, u32[]{:S(2)}) %collective-permute-start.37) | collective-permute-done | bytes 294944 | tf_op jit(solution)/shard_map/ppermute | solution.py:148
  394.3 57.2 %all_to_all.32 = f32[8,9,64,128]{3,2,1,0:T(8,128)S(1)} all-to-all(f32[8,9,64,128]{3,2,1,0:T(8,128)S(1)} %broadcast_select_fusion.4), channel_id=1, replica_groups=mesh['gx'=4,'gy'=8] {'gy'}, dimensions={0} | all-to-all | bytes 4718592 | tf_op jit(solution)/shard_map/all_to_all | solution.py:159
  491.3 4.3 collective-permute-start.29
  501.7 4.6 multiply_reduce_fusion.4
  521.4 4.3 collective-permute-start.49
  541.8 4.2 collective-permute-done.58
  567.5 6.9 collective-permute-done.59
  586.4 13.8 %collective-permute-done.61 = f32[1,1,9,64,128]{4,3,2,1,0:T(8,128)S(1)} collective-permute-done((f32[1,1,9,64,128]{4,3,2,1,0:T(8,128)S(1)}, f32[1,1,9,64,128]{4,3,2,1,0:T(8,128)S(1)}, u32[]{:S(2)}, u32[]{:S(2)}) %collective-permute-start.61) | collective-permute-done | bytes 294944 | tf_op jit(solution)/shard_map/ppermute | solution.py:148
  600.9 31.6 %collective-permute-done.62 = f32[1,1,9,64,128]{4,3,2,1,0:T(8,128)S(1)} collective-permute-done((f32[1,1,9,64,128]{4,3,2,1,0:T(8,128)S(1)}, f32[1,1,9,64,128]{4,3,2,1,0:T(8,128)S(1)}, u32[]{:S(2)}, u32[]{:S(2)}) %collective-permute-start.62) | collective-permute-done | bytes 294944 | tf_op jit(solution)/shard_map/ppermute | solution.py:148
  651.4 57.2 %all_to_all.33 = f32[8,9,64,128]{3,2,1,0:T(8,128)S(1)} all-to-all(f32[8,9,64,128]{3,2,1,0:T(8,128)S(1)} %broadcast_select_fusion.2), channel_id=1, replica_groups=mesh['gx'=4,'gy'=8] {'gy'}, dimensions={0} | all-to-all | bytes 4718592 | tf_op jit(solution)/shard_map/all_to_all | solution.py:159
  748.7 4.3 collective-permute-start.54
  759.2 5.2 multiply_reduce_fusion.2
  779.4 4.3 collective-permute-start.74
  825.6 6.9 collective-permute-done.84
  844.5 13.8 %collective-permute-done.86 = f32[1,1,9,64,128]{4,3,2,1,0:T(8,128)S(1)} collective-permute-done((f32[1,1,9,64,128]{4,3,2,1,0:T(8,128)S(1)}, f32[1,1,9,64,128]{4,3,2,1,0:T(8,128)S(1)}, u32[]{:S(2)}, u32[]{:S(2)}) %collective-permute-start.86) | collective-permute-done | bytes 294944 | tf_op jit(solution)/shard_map/ppermute | solution.py:148
  859.0 31.6 %collective-permute-done.87 = f32[1,1,9,64,128]{4,3,2,1,0:T(8,128)S(1)} collective-permute-done((f32[1,1,9,64,128]{4,3,2,1,0:T(8,128)S(1)}, f32[1,1,9,64,128]{4,3,2,1,0:T(8,128)S(1)}, u32[]{:S(2)}, u32[]{:S(2)}) %collective-permute-start.87) | collective-permute-done | bytes 294944 | tf_op jit(solution)/shard_map/ppermute | solution.py:148
  909.5 57.0 %all_to_all.34 = f32[8,9,64,128]{3,2,1,0:T(8,128)S(1)} all-to-all(f32[8,9,64,128]{3,2,1,0:T(8,128)S(1)} %broadcast_select_fusion), channel_id=1, replica_groups=mesh['gx'=4,'gy'=8] {'gy'}, dimensions={0} | all-to-all | bytes 4718592 | tf_op jit(solution)/shard_map/all_to_all | solution.py:159
  1006.8 4.3 collective-permute-start.79
  1017.3 4.5 multiply_reduce_fusion
  1036.8 4.3 collective-permute-start.99
  (434 shorter events, 506.0 us)
Async XLA Ops:
  13.6 15.6 %all-to-all-start = ((s32[8,1,9]{2,1,0:T(1,128)}), s32[8,1,9]{2,1,0:T(1,128)S(1)}, u32[]{:S(2)}, u32[]{:S(2)}) async-start(s32[8,1,9]{2,1,0:T(1,128)} %bitcast.4), calls=%async_computation | async-start | bytes 8192 | tf_op jit(solution)/shard_map/all_to_all | solution.py:122
  56.3 9.5 collective-permute-start.9
  68.2 23.6 %collective-permute-start.11 = (f32[1,1,9,64,128]{4,3,2,1,0:T(8,128)S(1)}, f32[1,1,9,64,128]{4,3,2,1,0:T(8,128)}, u32[]{:S(2)}, u32[]{:S(2)}) collective-permute-start(f32[1,1,9,64,128]{4,3,2,1,0:T(8,128)S(1)} %get-tuple-element.49), channel_id=1, source_target_pairs={{0,3},{1,4},{2,5},{3,6},{4,7},{5,0},{6,1},{7,2},{8,11},{9,12},{10,... | collective-permute-start | bytes 884744 | tf_op jit(solution)/shard_map/ppermute | solution.py:148
  70.4 56.1 %collective-permute-start.15 = (f32[1,1,9,64,128]{4,3,2,1,0:T(8,128)S(1)}, f32[1,1,9,64,128]{4,3,2,1,0:T(8,128)S(1)}, u32[]{:S(2)}, u32[]{:S(2)}) collective-permute-start(f32[1,1,9,64,128]{4,3,2,1,0:T(8,128)S(1)} %get-tuple-element.45), channel_id=1, source_target_pairs={{0,7},{1,0},{2,1},{3,2},{4,3},{5,4},{6,5},{7,6},{8,15},{9,8},{10,9... | collective-permute-start | bytes 884744 | tf_op jit(solution)/shard_map/ppermute | solution.py:148
  72.8 52.9 %collective-permute-start.14 = (f32[1,1,9,64,128]{4,3,2,1,0:T(8,128)S(1)}, f32[1,1,9,64,128]{4,3,2,1,0:T(8,128)S(1)}, u32[]{:S(2)}, u32[]{:S(2)}) collective-permute-start(f32[1,1,9,64,128]{4,3,2,1,0:T(8,128)S(1)} %get-tuple-element.46), channel_id=1, source_target_pairs={{0,6},{1,7},{2,0},{3,1},{4,2},{5,3},{6,4},{7,5},{8,14},{9,15},{10,... | collective-permute-start | bytes 884744 | tf_op jit(solution)/shard_map/ppermute | solution.py:148
  73.7 51.2 %collective-permute-start.13 = (f32[1,1,9,64,128]{4,3,2,1,0:T(8,128)S(1)}, f32[1,1,9,64,128]{4,3,2,1,0:T(8,128)S(1)}, u32[]{:S(2)}, u32[]{:S(2)}) collective-permute-start(f32[1,1,9,64,128]{4,3,2,1,0:T(8,128)S(1)} %get-tuple-element.47), channel_id=1, source_target_pairs={{0,5},{1,6},{2,7},{3,0},{4,1},{5,2},{6,3},{7,4},{8,13},{9,14},{10,... | collective-permute-start | bytes 884744 | tf_op jit(solution)/shard_map/ppermute | solution.py:148
  77.0 47.2 %collective-permute-start.12 = (f32[1,1,9,64,128]{4,3,2,1,0:T(8,128)S(1)}, f32[1,1,9,64,128]{4,3,2,1,0:T(8,128)S(1)}, u32[]{:S(2)}, u32[]{:S(2)}) collective-permute-start(f32[1,1,9,64,128]{4,3,2,1,0:T(8,128)S(1)} %get-tuple-element.48), channel_id=1, source_target_pairs={{0,4},{1,5},{2,6},{3,7},{4,0},{5,1},{6,2},{7,3},{8,12},{9,13},{10,... | collective-permute-start | bytes 884744 | tf_op jit(solution)/shard_map/ppermute | solution.py:148
  144.5 58.8 %all-to-all-start.1 = ((f32[8,9,64,128]{3,2,1,0:T(8,128)}), f32[8,9,64,128]{3,2,1,0:T(8,128)}, u32[]{:S(2)}, u32[]{:S(2)}) async-start(f32[8,9,64,128]{3,2,1,0:T(8,128)} %broadcast_select_fusion.6), calls=%async_computation.1 | async-start | bytes 4718592 | tf_op jit(solution)/shard_map/all_to_all | solution.py:159
  307.9 9.5 collective-permute-start.34
  319.6 23.9 %collective-permute-start.36 = (f32[1,1,9,64,128]{4,3,2,1,0:T(8,128)S(1)}, f32[1,1,9,64,128]{4,3,2,1,0:T(8,128)S(1)}, u32[]{:S(2)}, u32[]{:S(2)}) collective-permute-start(f32[1,1,9,64,128]{4,3,2,1,0:T(8,128)S(1)} %get-tuple-element.42), channel_id=1, source_target_pairs={{0,3},{1,4},{2,5},{3,6},{4,7},{5,0},{6,1},{7,2},{8,11},{9,12},{10,... | collective-permute-start | bytes 884744 | tf_op jit(solution)/shard_map/ppermute | solution.py:148
  322.1 55.6 %collective-permute-start.40 = (f32[1,1,9,64,128]{4,3,2,1,0:T(8,128)S(1)}, f32[1,1,9,64,128]{4,3,2,1,0:T(8,128)S(1)}, u32[]{:S(2)}, u32[]{:S(2)}) collective-permute-start(f32[1,1,9,64,128]{4,3,2,1,0:T(8,128)S(1)} %get-tuple-element.38), channel_id=1, source_target_pairs={{0,7},{1,0},{2,1},{3,2},{4,3},{5,4},{6,5},{7,6},{8,15},{9,8},{10,9... | collective-permute-start | bytes 884744 | tf_op jit(solution)/shard_map/ppermute | solution.py:148
  323.9 53.1 %collective-permute-start.39 = (f32[1,1,9,64,128]{4,3,2,1,0:T(8,128)S(1)}, f32[1,1,9,64,128]{4,3,2,1,0:T(8,128)S(1)}, u32[]{:S(2)}, u32[]{:S(2)}) collective-permute-start(f32[1,1,9,64,128]{4,3,2,1,0:T(8,128)S(1)} %get-tuple-element.39), channel_id=1, source_target_pairs={{0,6},{1,7},{2,0},{3,1},{4,2},{5,3},{6,4},{7,5},{8,14},{9,15},{10,... | collective-permute-start | bytes 884744 | tf_op jit(solution)/shard_map/ppermute | solution.py:148
  324.9 51.3 %collective-permute-start.38 = (f32[1,1,9,64,128]{4,3,2,1,0:T(8,128)S(1)}, f32[1,1,9,64,128]{4,3,2,1,0:T(8,128)S(1)}, u32[]{:S(2)}, u32[]{:S(2)}) collective-permute-start(f32[1,1,9,64,128]{4,3,2,1,0:T(8,128)S(1)} %get-tuple-element.40), channel_id=1, source_target_pairs={{0,5},{1,6},{2,7},{3,0},{4,1},{5,2},{6,3},{7,4},{8,13},{9,14},{10,... | collective-permute-start | bytes 884744 | tf_op jit(solution)/shard_map/ppermute | solution.py:148
  328.2 47.2 %collective-permute-start.37 = (f32[1,1,9,64,128]{4,3,2,1,0:T(8,128)S(1)}, f32[1,1,9,64,128]{4,3,2,1,0:T(8,128)S(1)}, u32[]{:S(2)}, u32[]{:S(2)}) collective-permute-start(f32[1,1,9,64,128]{4,3,2,1,0:T(8,128)S(1)} %get-tuple-element.41), channel_id=1, source_target_pairs={{0,4},{1,5},{2,6},{3,7},{4,0},{5,1},{6,2},{7,3},{8,12},{9,13},{10,... | collective-permute-start | bytes 884744 | tf_op jit(solution)/shard_map/ppermute | solution.py:148
  469.6 26.9 %collective-permute-start.43 = (f32[4,264,4]{1,2,0:T(4,128)S(1)}, f32[4,264,4]{1,2,0:T(4,128)S(1)}, u32[]{:S(2)}, u32[]{:S(2)}) collective-permute-start(f32[4,264,4]{1,2,0:T(4,128)S(1)} %copy.37), channel_id=1, source_target_pairs={{0,1},{1,2},{2,3},{3,4},{4,5},{5,6},{6,7},{8,9},{9,10},{10,11},{11... | collective-permute-start | bytes 50696 | tf_op jit(solution)/shard_map/ppermute | solution.py:34
  473.3 23.5 %collective-permute-start.44 = (f32[4,264,4]{1,2,0:T(4,128)S(1)}, f32[4,264,4]{1,2,0:T(4,128)S(1)}, u32[]{:S(2)}, u32[]{:S(2)}) collective-permute-start(f32[4,264,4]{1,2,0:T(4,128)S(1)} %copy.38), channel_id=1, source_target_pairs={{1,0},{2,1},{3,2},{4,3},{5,4},{6,5},{7,6},{9,8},{10,9},{11,10},{12... | collective-permute-start | bytes 50696 | tf_op jit(solution)/shard_map/ppermute | solution.py:37
  564.9 9.5 collective-permute-start.59
  576.7 23.5 %collective-permute-start.61 = (f32[1,1,9,64,128]{4,3,2,1,0:T(8,128)S(1)}, f32[1,1,9,64,128]{4,3,2,1,0:T(8,128)S(1)}, u32[]{:S(2)}, u32[]{:S(2)}) collective-permute-start(f32[1,1,9,64,128]{4,3,2,1,0:T(8,128)S(1)} %get-tuple-element.35), channel_id=1, source_target_pairs={{0,3},{1,4},{2,5},{3,6},{4,7},{5,0},{6,1},{7,2},{8,11},{9,12},{10,... | collective-permute-start | bytes 884744 | tf_op jit(solution)/shard_map/ppermute | solution.py:148
  578.0 56.7 %collective-permute-start.65 = (f32[1,1,9,64,128]{4,3,2,1,0:T(8,128)S(1)}, f32[1,1,9,64,128]{4,3,2,1,0:T(8,128)S(1)}, u32[]{:S(2)}, u32[]{:S(2)}) collective-permute-start(f32[1,1,9,64,128]{4,3,2,1,0:T(8,128)S(1)} %get-tuple-element.31), channel_id=1, source_target_pairs={{0,7},{1,0},{2,1},{3,2},{4,3},{5,4},{6,5},{7,6},{8,15},{9,8},{10,9... | collective-permute-start | bytes 884744 | tf_op jit(solution)/shard_map/ppermute | solution.py:148
  580.8 53.2 %collective-permute-start.64 = (f32[1,1,9,64,128]{4,3,2,1,0:T(8,128)S(1)}, f32[1,1,9,64,128]{4,3,2,1,0:T(8,128)S(1)}, u32[]{:S(2)}, u32[]{:S(2)}) collective-permute-start(f32[1,1,9,64,128]{4,3,2,1,0:T(8,128)S(1)} %get-tuple-element.32), channel_id=1, source_target_pairs={{0,6},{1,7},{2,0},{3,1},{4,2},{5,3},{6,4},{7,5},{8,14},{9,15},{10,... | collective-permute-start | bytes 884744 | tf_op jit(solution)/shard_map/ppermute | solution.py:148
  582.0 51.3 %collective-permute-start.63 = (f32[1,1,9,64,128]{4,3,2,1,0:T(8,128)S(1)}, f32[1,1,9,64,128]{4,3,2,1,0:T(8,128)S(1)}, u32[]{:S(2)}, u32[]{:S(2)}) collective-permute-start(f32[1,1,9,64,128]{4,3,2,1,0:T(8,128)S(1)} %get-tuple-element.33), channel_id=1, source_target_pairs={{0,5},{1,6},{2,7},{3,0},{4,1},{5,2},{6,3},{7,4},{8,13},{9,14},{10,... | collective-permute-start | bytes 884744 | tf_op jit(solution)/shard_map/ppermute | solution.py:148
  585.3 47.2 %collective-permute-start.62 = (f32[1,1,9,64,128]{4,3,2,1,0:T(8,128)S(1)}, f32[1,1,9,64,128]{4,3,2,1,0:T(8,128)S(1)}, u32[]{:S(2)}, u32[]{:S(2)}) collective-permute-start(f32[1,1,9,64,128]{4,3,2,1,0:T(8,128)S(1)} %get-tuple-element.34), channel_id=1, source_target_pairs={{0,4},{1,5},{2,6},{3,7},{4,0},{5,1},{6,2},{7,3},{8,12},{9,13},{10,... | collective-permute-start | bytes 884744 | tf_op jit(solution)/shard_map/ppermute | solution.py:148
  726.7 27.2 %collective-permute-start.68 = (f32[4,264,4]{1,2,0:T(4,128)S(1)}, f32[4,264,4]{1,2,0:T(4,128)S(1)}, u32[]{:S(2)}, u32[]{:S(2)}) collective-permute-start(f32[4,264,4]{1,2,0:T(4,128)S(1)} %copy.47), channel_id=1, source_target_pairs={{0,1},{1,2},{2,3},{3,4},{4,5},{5,6},{6,7},{8,9},{9,10},{10,11},{11... | collective-permute-start | bytes 50696 | tf_op jit(solution)/shard_map/ppermute | solution.py:34
  730.4 23.8 %collective-permute-start.69 = (f32[4,264,4]{1,2,0:T(4,128)S(1)}, f32[4,264,4]{1,2,0:T(4,128)S(1)}, u32[]{:S(2)}, u32[]{:S(2)}) collective-permute-start(f32[4,264,4]{1,2,0:T(4,128)S(1)} %copy.48), channel_id=1, source_target_pairs={{1,0},{2,1},{3,2},{4,3},{5,4},{6,5},{7,6},{9,8},{10,9},{11,10},{12... | collective-permute-start | bytes 50696 | tf_op jit(solution)/shard_map/ppermute | solution.py:37
  823.0 9.5 collective-permute-start.84
  834.7 23.5 %collective-permute-start.86 = (f32[1,1,9,64,128]{4,3,2,1,0:T(8,128)S(1)}, f32[1,1,9,64,128]{4,3,2,1,0:T(8,128)S(1)}, u32[]{:S(2)}, u32[]{:S(2)}) collective-permute-start(f32[1,1,9,64,128]{4,3,2,1,0:T(8,128)S(1)} %get-tuple-element.28), channel_id=1, source_target_pairs={{0,3},{1,4},{2,5},{3,6},{4,7},{5,0},{6,1},{7,2},{8,11},{9,12},{10,... | collective-permute-start | bytes 884744 | tf_op jit(solution)/shard_map/ppermute | solution.py:148
  836.1 56.7 %collective-permute-start.90 = (f32[1,1,9,64,128]{4,3,2,1,0:T(8,128)S(1)}, f32[1,1,9,64,128]{4,3,2,1,0:T(8,128)S(1)}, u32[]{:S(2)}, u32[]{:S(2)}) collective-permute-start(f32[1,1,9,64,128]{4,3,2,1,0:T(8,128)S(1)} %get-tuple-element.24), channel_id=1, source_target_pairs={{0,7},{1,0},{2,1},{3,2},{4,3},{5,4},{6,5},{7,6},{8,15},{9,8},{10,9... | collective-permute-start | bytes 884744 | tf_op jit(solution)/shard_map/ppermute | solution.py:148
  838.8 53.2 %collective-permute-start.89 = (f32[1,1,9,64,128]{4,3,2,1,0:T(8,128)S(1)}, f32[1,1,9,64,128]{4,3,2,1,0:T(8,128)S(1)}, u32[]{:S(2)}, u32[]{:S(2)}) collective-permute-start(f32[1,1,9,64,128]{4,3,2,1,0:T(8,128)S(1)} %get-tuple-element.25), channel_id=1, source_target_pairs={{0,6},{1,7},{2,0},{3,1},{4,2},{5,3},{6,4},{7,5},{8,14},{9,15},{10,... | collective-permute-start | bytes 884744 | tf_op jit(solution)/shard_map/ppermute | solution.py:148
  840.0 51.3 %collective-permute-start.88 = (f32[1,1,9,64,128]{4,3,2,1,0:T(8,128)S(1)}, f32[1,1,9,64,128]{4,3,2,1,0:T(8,128)S(1)}, u32[]{:S(2)}, u32[]{:S(2)}) collective-permute-start(f32[1,1,9,64,128]{4,3,2,1,0:T(8,128)S(1)} %get-tuple-element.26), channel_id=1, source_target_pairs={{0,5},{1,6},{2,7},{3,0},{4,1},{5,2},{6,3},{7,4},{8,13},{9,14},{10,... | collective-permute-start | bytes 884744 | tf_op jit(solution)/shard_map/ppermute | solution.py:148
  843.4 47.2 %collective-permute-start.87 = (f32[1,1,9,64,128]{4,3,2,1,0:T(8,128)S(1)}, f32[1,1,9,64,128]{4,3,2,1,0:T(8,128)S(1)}, u32[]{:S(2)}, u32[]{:S(2)}) collective-permute-start(f32[1,1,9,64,128]{4,3,2,1,0:T(8,128)S(1)} %get-tuple-element.27), channel_id=1, source_target_pairs={{0,4},{1,5},{2,6},{3,7},{4,0},{5,1},{6,2},{7,3},{8,12},{9,13},{10,... | collective-permute-start | bytes 884744 | tf_op jit(solution)/shard_map/ppermute | solution.py:148
  984.6 27.5 %collective-permute-start.93 = (f32[4,264,4]{1,2,0:T(4,128)S(1)}, f32[4,264,4]{1,2,0:T(4,128)S(1)}, u32[]{:S(2)}, u32[]{:S(2)}) collective-permute-start(f32[4,264,4]{1,2,0:T(4,128)S(1)} %copy.57), channel_id=1, source_target_pairs={{0,1},{1,2},{2,3},{3,4},{4,5},{5,6},{6,7},{8,9},{9,10},{10,11},{11... | collective-permute-start | bytes 50696 | tf_op jit(solution)/shard_map/ppermute | solution.py:34
  988.2 24.1 %collective-permute-start.94 = (f32[4,264,4]{1,2,0:T(4,128)S(1)}, f32[4,264,4]{1,2,0:T(4,128)S(1)}, u32[]{:S(2)}, u32[]{:S(2)}) collective-permute-start(f32[4,264,4]{1,2,0:T(4,128)S(1)} %copy.58), channel_id=1, source_target_pairs={{1,0},{2,1},{3,2},{4,3},{5,4},{6,5},{7,6},{9,8},{10,9},{11,10},{12... | collective-permute-start | bytes 50696 | tf_op jit(solution)/shard_map/ppermute | solution.py:37
  (106 other events, 822.0 us)
